TPU v7x, 128 devices: a whole 4x4x4 slice. The times are simulated.
128 devices in a mesh: gx: 4 (over z), gy: 32 (over y, x, core).
Axes of the slice: x: 4, y: 4, z: 4, core: 2. Of those that a mesh axis runs over, the one named last changes fastest.
Arguments:
- tokens: bfloat16 [32768, 1664], P('gy', 'gx'), may hold values from -6 to 6
- segment_ids: int32 [32768], P('gy'), may hold values from 0 to 1023, as said below
- first_gain: float32 [1664], replicated, may hold values from 0.5 to 2
- first_bias: float32 [1664], replicated, may hold values from -3 to 3
- query_key_value: bfloat16 [3, 1664, 1664], P(None, 'gy', 'gx'), may hold values from -0.15625 to 0.15625
- project_out: bfloat16 [1664, 1664], P('gx', 'gy'), may hold values from -0.15625 to 0.15625
- second_gain: float32 [1664], replicated, may hold values from 0.5 to 2
- second_bias: float32 [1664], replicated, may hold values from -3 to 3
- up_weight: bfloat16 [1664, 8192], P('gy', 'gx'), may hold values from -0.15625 to 0.15625
- down_weight: bfloat16 [8192, 1664], P('gx', 'gy'), may hold values from -0.0625 to 0.0625
- final_gain: float32 [1664], replicated, may hold values from 0.5 to 2
- final_bias: float32 [1664], replicated, may hold values from -3 to 3
- merge_weight: bfloat16 [4, 1664, 1664], P(None, 'gx', 'gy'), may hold values from -0.078125 to 0.078125
- owners: int32 [8192, 1], P('gy'), may hold values from 0 to 31; in each aligned block of 256 rows (0 to 255, 256 to 511, ...) at most 16 rows name the same one
Outputs:
- delivered: bfloat16 [32, 32, 16, 1664], P('gy', None, None, 'gx')
Inputs may be any that keep to these rules, and one draw needn't show every extreme that they name: `segment_ids`: each segment is a run of whole units of 32 consecutive tokens that lies inside one aligned block of 1024 tokens; ids never fall along the tokens and differ between segments. `owners`: in each aligned block of 256 rows (the merged tokens of one index of gy), no owner is named by more than 16 rows.
All inputs are finite; a program needn't handle non-finite values.
Results may differ from a plain program's by a relative error of at most 0.02.
Values may be sent and summed in bfloat16 or wider, within the bound.
No kernel may reach another device: no remote copies, remote signals or barrier semaphores. Data moves between devices by JAX's collectives and lax.ppermute only.
A program may use at most 128 MiB of HBM per device.

v0:
```python
import jax
import jax.numpy as jnp
from jax import lax
from jax.sharding import PartitionSpec as P

HEAD = 104
IMG_W = 16
EPSILON = 1e-06


def normalize_rows(values, gain, bias):
    values = values.astype(jnp.float32)
    center = values - jnp.mean(values, axis=-1, keepdims=True)
    spread = jnp.mean(center * center, axis=-1, keepdims=True)
    return center * lax.rsqrt(spread + EPSILON) * gain + bias


def normalize_from_sums(values, sums, features, gain, bias):
    values = values.astype(jnp.float32)
    row_mean = sums[0] / features
    spread = sums[1] / features - row_mean * row_mean
    return (values - row_mean[:, None]) * lax.rsqrt(spread[:, None] + EPSILON) * gain + bias


def own_slice(vector, width):
    return lax.dynamic_slice_in_dim(vector, lax.axis_index("gx") * width, width, 0)


def row_sums(values):
    values = values.astype(jnp.float32)
    return (jnp.sum(values, axis=-1), jnp.sum(values * values, axis=-1))


def local_attention(qkv, segment_ids):
    tok_rows = qkv.shape[1]
    head_count = qkv.shape[2] // HEAD
    queries = qkv[0].reshape(tok_rows, head_count, HEAD)
    key_rows = qkv[1].reshape(tok_rows, head_count, HEAD)
    value_rows = qkv[2].reshape(tok_rows, head_count, HEAD)
    query_block = min(512, tok_rows)

    def one_block(index):
        first_query = index * query_block
        query_part = lax.dynamic_slice_in_dim(queries, first_query, query_block, 0)
        query_ids = lax.dynamic_slice_in_dim(segment_ids, first_query, query_block, 0)
        scores = jnp.einsum(
            "qhe,khe->hqk", query_part, key_rows, preferred_element_type=jnp.float32
        ) * HEAD ** (-0.5)
        same_segment = query_ids[None, :, None] == segment_ids[None, None, :]
        scores = jnp.where(same_segment, scores, -1e30)
        highest = jnp.max(scores, axis=-1, keepdims=True)
        raised = jnp.exp(scores - highest)
        shares = (raised / jnp.sum(raised, axis=-1, keepdims=True)).astype(jnp.bfloat16)
        return jnp.einsum(
            "hqk,khe->qhe", shares, value_rows, preferred_element_type=jnp.float32
        ).astype(jnp.bfloat16)

    blocks = lax.map(one_block, jnp.arange(tok_rows // query_block, dtype=jnp.int32))
    return blocks.reshape(tok_rows, head_count * HEAD)


def body(
    tokens,
    segment_ids,
    first_gain,
    first_bias,
    query_key_value,
    project_out,
    second_gain,
    second_bias,
    up_weight,
    down_weight,
    final_gain,
    final_bias,
    merge_weight,
    owners,
):
    tok_rows = tokens.shape[0]
    feature_cols = tokens.shape[1]
    features = feature_cols * lax.axis_size("gx")
    full_rows = lax.all_gather(tokens, "gx", axis=1, tiled=True)
    normed = normalize_rows(full_rows, first_gain, first_bias).astype(jnp.bfloat16)
    columns = normed
    qkv = jnp.einsum(
        "td,kdc->ktc",
        columns,
        lax.all_gather(query_key_value, "gy", axis=1, tiled=True),
        preferred_element_type=jnp.float32,
    ).astype(jnp.bfloat16)
    attended = local_attention(qkv, segment_ids)
    out_terms = jnp.dot(
        attended,
        lax.all_gather(project_out, "gy", axis=1, tiled=True),
        preferred_element_type=jnp.float32,
    )
    attn_share = lax.psum_scatter(
        out_terms.astype(jnp.bfloat16), "gx", scatter_dimension=1, tiled=True
    ).astype(jnp.float32)
    first_resid = (tokens.astype(jnp.float32) + attn_share).astype(jnp.bfloat16)
    resid_rows = lax.all_gather(first_resid, "gx", axis=1, tiled=True)
    second_normed = normalize_rows(resid_rows, second_gain, second_bias).astype(jnp.bfloat16)
    columns = second_normed
    upper = jnp.dot(
        columns,
        lax.all_gather(up_weight, "gy", axis=0, tiled=True),
        preferred_element_type=jnp.float32,
    )
    hidden = jax.nn.gelu(upper, approximate=False).astype(jnp.bfloat16)
    down_terms = jnp.dot(
        hidden,
        lax.all_gather(down_weight, "gy", axis=1, tiled=True),
        preferred_element_type=jnp.float32,
    )
    mlp_share = lax.psum_scatter(
        down_terms.astype(jnp.bfloat16), "gx", scatter_dimension=1, tiled=True
    ).astype(jnp.float32)
    second_resid = (first_resid.astype(jnp.float32) + mlp_share).astype(jnp.bfloat16)
    post_sums = lax.psum(row_sums(second_resid), "gx")
    final_normed = normalize_from_sums(
        second_resid,
        post_sums,
        features,
        own_slice(final_gain, feature_cols),
        own_slice(final_bias, feature_cols),
    ).astype(jnp.bfloat16)
    merged_rows = tok_rows // 4
    grouped = (
        final_normed.reshape(tok_rows // (2 * IMG_W), 2, IMG_W // 2, 2, feature_cols)
        .transpose(0, 2, 1, 3, 4)
        .reshape(merged_rows, 4, feature_cols)
    )
    merge_terms = jnp.einsum(
        "pkf,kfc->pc",
        grouped,
        lax.all_gather(merge_weight, "gy", axis=2, tiled=True),
        preferred_element_type=jnp.float32,
    )
    projected = lax.psum_scatter(
        merge_terms.astype(jnp.bfloat16), "gx", scatter_dimension=1, tiled=True
    )
    owner_count = lax.axis_size("gy")
    capacity = max(2, 2 * merged_rows // owner_count)
    owner_col = owners[:, 0]
    one_hot = (owner_col[:, None] == jnp.arange(owner_count, dtype=jnp.int32)[None, :]).astype(
        jnp.int32
    )
    slot_rank = jnp.sum((jnp.cumsum(one_hot, axis=0) - 1) * one_hot, axis=1)
    outgoing = (
        jnp.zeros((owner_count, capacity, feature_cols), jnp.bfloat16)
        .at[owner_col, slot_rank]
        .set(projected)
    )
    arrived = lax.all_to_all(outgoing, "gy", split_axis=0, concat_axis=0, tiled=True)
    return arrived.reshape(1, owner_count, capacity, feature_cols)


def solution(mesh):
    in_specs = (
        P("gy", "gx"),
        P("gy"),
        P(),
        P(),
        P(None, "gy", "gx"),
        P("gx", "gy"),
        P(),
        P(),
        P("gy", "gx"),
        P("gx", "gy"),
        P(),
        P(),
        P(None, "gx", "gy"),
        P("gy", None),
    )
    out_specs = P("gy", None, None, "gx")
    return jax.shard_map(body, mesh=mesh, in_specs=in_specs, out_specs=out_specs, check_vma=False)
```

profile of v0, /device:TPU:1, one launch (start us, length us, event | category | flops | bytes accessed | tf_op | source)
XLA Modules:
  0.0 590.1 jit_solution(16521097210101806304)
XLA Ops:
  6.5 0.7 all-gather.19.cloned.1.call-update
  7.3 0.7 all-gather.11.cloned.1.call-update
  8.1 1.7 copy.27
  9.9 46.5 %all-gather.19.cloned.1.call-done = bf16[32,52,416]{2,1,0:T(8,128)(2,1)} async-done(((bf16[1,52,416]{2,1,0:T(8,128)(2,1)}), bf16[32,52,416]{2,1,0:T(8,128)(2,1)}) %all-gather.19.cloned.1.call-update) | async-done | bytes 1384464 | tf_op jit(solution)/shard_map/all_gather | solution.py:93
  56.4 3.9 reshape.125
  60.2 38.4 %all-gather.11.cloned.1.call-done = bf16[1024,1664]{0,1:T(8,128)(2,1)} async-done(((bf16[1024,416]{0,1:T(8,128)(2,1)}), bf16[1024,1664]{0,1:T(8,128)(2,1)}) %all-gather.11.cloned.1.call-update) | async-done | bytes 3407888 | tf_op jit(solution)/shard_map/all_gather | solution.py:81
  98.7 2.7 convert_reduce_fusion.1
  101.4 2.9 fusion.42
  104.3 47.0 %all-gather.13.cloned.1.call-done = bf16[3,1664,416]{2,0,1:T(4,128)(2,1)} async-done(((bf16[3,52,416]{2,0,1:T(4,128)(2,1)}), bf16[3,1664,416]{2,0,1:T(4,128)(2,1)}) %all-gather.13.cloned.1.call-update) | async-done | bytes 4153360 | tf_op jit(solution)/shard_map/all_gather | solution.py:87
  151.3 8.7 %convert_bitcast_fusion = bf16[3,1024,416]{1,2,0:T(8,128)(2,1)S(1)} fusion(bf16[3,1664,416]{2,0,1:T(4,128)(2,1)} %all-gather.13.cloned.1.call-done, bf16[1024,1664]{0,1:T(8,128)(2,1)S(1)} %copy-done.1, f32[1664]{0:T(1024)S(1)} %copy-done.7, f32[1664]{0:T(1024)S(1)} %copy-done.8, f32[1024]{0:T(1024)S(1)} %add_rsqrt_fusion.2, ...), kind=kOutput, calls=%fused_computation.79 | convolution fusion | flops 4264525824 | bytes 10138624 | tf_op jit(solution)/shard_map/td,kdc->ktc/dot_general | solution.py:84
  160.0 1.5 fusion.129
  161.5 30.1 %while.10 = (s32[]{:T(128)}, bf16[2,512,4,104]{1,3,2,0:T(8,128)(2,1)}, s32[2]{0:T(128)S(1)}, s32[1024]{0:T(1024)S(1)}, bf16[1024,4,104]{0,2,1:T(8,128)(2,1)}, /*...) while((s32[]{:T(128)}, ...), condition=%wide.region_8.9_spmd, body=%wide.region_5.8_spmd.sunk | while | flops 885736448 | bytes 20409008 | solution.py:58
  161.7 0.6 dynamic_slice.34
  163.4 7.6 %fusion.157 = (f32[4,512]{1,0:T(4,128)S(1)}, f32[4,512,1024]{2,1,0:T(8,128)}) fusion(pred[512,1024]{1,0:T(8,128)(4,1)S(1)} %broadcast_compare_fusion.2, bf16[1024,4,104]{0,2,1:T(8,128)(2,1)} %get-tuple-element.142, bf16[1024,4,104]{0,2,1:T(8,128)(2,1)} %get-tuple-element.141, s32[]{:T(128)S(6)} %select_n.48), kind=kOutput, calls=%fused_computation.137.clone.1 | convolution fusion | flops 444597248 | bytes 10199044 | tf_op jit(solution)/shard_map/while/body/eval_jaxpr/sub | solution.py:52
  171.0 5.7 fusion.158
  176.6 0.6 dynamic_slice.34
  178.3 7.6 %fusion.157 = (f32[4,512]{1,0:T(4,128)S(1)}, f32[4,512,1024]{2,1,0:T(8,128)}) fusion(pred[512,1024]{1,0:T(8,128)(4,1)S(1)} %broadcast_compare_fusion.2, bf16[1024,4,104]{0,2,1:T(8,128)(2,1)} %get-tuple-element.142, bf16[1024,4,104]{0,2,1:T(8,128)(2,1)} %get-tuple-element.141, s32[]{:T(128)S(6)} %select_n.48), kind=kOutput, calls=%fused_computation.137.clone.1 | convolution fusion | flops 444597248 | bytes 10199044 | tf_op jit(solution)/shard_map/while/body/eval_jaxpr/sub | solution.py:52
  185.9 5.7 fusion.158
  191.6 2.0 copy.30
  193.8 3.7 convolution_convert_fusion
  197.6 0.5 all-gather.21.cloned.1.call-update
  198.7 38.0 %reduce-scatter.4.cloned.1.call-done = bf16[1024,416]{0,1:T(8,128)(2,1)} async-done(((bf16[1024,1664]{0,1:T(8,128)(2,1)}), bf16[1024,416]{0,1:T(8,128)(2,1)}) %reduce-scatter.4.cloned.1.call-update) | async-done | bytes 851984 | tf_op jit(solution)/shard_map/reduce_scatter | solution.py:96
  236.8 2.5 add_convert_fusion.1
  239.3 50.2 %all-gather.21.cloned.1.call-done = bf16[32,52,2048]{2,1,0:T(8,128)(2,1)} async-done(((bf16[1,52,2048]{2,1,0:T(8,128)(2,1)}), bf16[32,52,2048]{2,1,0:T(8,128)(2,1)}) %all-gather.21.cloned.1.call-update) | async-done | bytes 6815760 | tf_op jit(solution)/shard_map/all_gather | solution.py:105
  289.5 8.6 %reshape.127 = bf16[1664,2048]{1,0:T(8,128)(2,1)} reshape(bf16[32,52,2048]{2,1,0:T(8,128)(2,1)} %all-gather.21.cloned.1.call-done) | data formatting | bytes 13631488
  298.1 43.3 %all-gather.23.cloned.1.call-done = bf16[32,52,2048]{2,1,0:T(8,128)(2,1)} async-done(((bf16[1,52,2048]{2,1,0:T(8,128)(2,1)}), bf16[32,52,2048]{2,1,0:T(8,128)(2,1)}) %all-gather.23.cloned.1.call-update) | async-done | bytes 6815760 | tf_op jit(solution)/shard_map/all_gather | solution.py:111
  341.5 8.8 %reshape.129 = bf16[1664,2048]{1,0:T(8,128)(2,1)} reshape(bf16[32,52,2048]{2,1,0:T(8,128)(2,1)} %all-gather.23.cloned.1.call-done) | data formatting | bytes 13631488
  350.3 33.4 %all-gather.15.cloned.1.call-done = bf16[1024,1664]{0,1:T(8,128)(2,1)} async-done(((bf16[1024,416]{0,1:T(8,128)(2,1)}), bf16[1024,1664]{0,1:T(8,128)(2,1)}) %all-gather.15.cloned.1.call-update) | async-done | bytes 3407888 | tf_op jit(solution)/shard_map/all_gather | solution.py:100
  383.7 2.7 convert_reduce_fusion
  386.4 3.1 fusion.38
  389.5 29.4 %fusion.147 = bf16[1024,2048]{1,0:T(8,128)(2,1)S(1)} fusion(bf16[1664,2048]{1,0:T(8,128)(2,1)} %reshape.127, bf16[1024,1664]{0,1:T(8,128)(2,1)S(1)} %copy-done.2, f32[1664]{0:T(1024)S(1)} %copy-done.9, f32[1664]{0:T(1024)S(1)} %copy-done.10, f32[1024]{0:T(1024)S(1)} %add_rsqrt_fusion.1, f32[1024]{0:T(1024)S(1)} %broadcast_multiply_fusion.1), kind=kOutput, calls=%fused_computation.29.clone.clone.clone.clone.1 | convolution fusion | flops 7125860352 | bytes 14439424 | tf_op jit(solution)/shard_map/dot_general | solution.py:103
  419.0 8.7 %fusion.52 = bf16[1024,1664]{0,1:T(8,128)(2,1)} fusion(bf16[1664,2048]{1,0:T(8,128)(2,1)S(1)} %bitcast.78, bf16[1024,2048]{1,0:T(8,128)(2,1)S(1)} %fusion.147), kind=kOutput, calls=%fused_computation.62 | convolution fusion | flops 6981025792 | bytes 14417920 | tf_op jit(solution)/shard_map/dot_general | solution.py:109
  427.8 0.7 all-gather.17.cloned.1.call-update
  428.5 0.8 dynamic_slice.16
  429.3 0.8 dynamic_slice.17
  430.1 38.6 %reduce-scatter.6.cloned.1.call-done = bf16[1024,416]{0,1:T(8,128)(2,1)} async-done(((bf16[1024,1664]{0,1:T(8,128)(2,1)}), bf16[1024,416]{0,1:T(8,128)(2,1)}) %reduce-scatter.6.cloned.1.call-update) | async-done | bytes 851984 | tf_op jit(solution)/shard_map/reduce_scatter | solution.py:114
  468.7 1.5 convert_reduce_fusion.2
  470.2 6.6 %all-reduce = (f32[1024]{0:T(1024)S(1)}, f32[1024]{0:T(1024)S(1)}) all-reduce(f32[1024]{0:T(1024)S(1)} %get-tuple-element.44, f32[1024]{0:T(1024)S(1)} %get-tuple-element.43), channel_id=1, replica_groups=mesh['gx'=4,'gy'=32] {'gx'}, use_global_device_ids=true, to_apply=%region_16.17 | all-reduce | flops 2048 | bytes 16384 | tf_op jit(solution)/shard_map/psum | solution.py:118
  476.8 1.6 fusion.88
  478.4 0.7 copy.31
  479.9 40.9 %all-gather.17.cloned.1.call-done = bf16[4,416,1664]{1,0,2:T(4,128)(2,1)} async-done(((bf16[4,416,52]{1,0,2:T(4,128)(2,1)}), bf16[4,416,1664]{1,0,2:T(4,128)(2,1)}) %all-gather.17.cloned.1.call-update) | async-done | bytes 5537808 | tf_op jit(solution)/shard_map/all_gather | solution.py:135
  520.8 6.3 %fusion.78 = bf16[256,1664]{0,1:T(8,128)(2,1)} fusion(bf16[256,4,416]{2,0,1:T(8,128)(2,1)S(1)} %bitcast.82, bf16[4,416,1664]{1,0,2:T(4,128)(2,1)} %all-gather.17.cloned.1.call-done), kind=kOutput, calls=%fused_computation.75 | convolution fusion | flops 1418100736 | bytes 7241728 | tf_op jit(solution)/shard_map/pkf,kfc->pc/dot_general | solution.py:132
  527.1 0.6 reduce-window.6
  528.1 19.4 %reduce-scatter.8.cloned.1.call-done = bf16[256,416]{0,1:T(8,128)(2,1)} async-done(((bf16[256,1664]{0,1:T(8,128)(2,1)}), bf16[256,416]{0,1:T(8,128)(2,1)}) %reduce-scatter.8.cloned.1.call-update) | async-done | bytes 213008 | tf_op jit(solution)/shard_map/reduce_scatter | solution.py:138
  547.5 1.1 copy.35
  548.7 13.6 %scatter_fusion = bf16[32,16,416]{2,1,0:T(8,128)(2,1)S(1)} fusion(bf16[32,16,416]{2,1,0:T(8,128)(2,1)S(1)} %broadcast_in_dim.24, s32[256]{0:T(256)S(1)} %bitcast.76, bf16[256,416]{1,0:T(8,128)(2,1)S(1)} %copy.35), kind=kCustom, calls=%fused_computation | custom fusion | bytes 641024 | tf_op jit(solution)/shard_map/scatter | solution.py:151
  562.3 20.0 %all_to_all.5 = bf16[32,16,416]{2,1,0:T(8,128)(2,1)S(1)} all-to-all(bf16[32,16,416]{2,1,0:T(8,128)(2,1)S(1)} %scatter_fusion), channel_id=1, replica_groups=mesh['gx'=4,'gy'=32] {'gy'}, dimensions={0} | all-to-all | bytes 851968 | tf_op jit(solution)/shard_map/all_to_all | solution.py:153
  582.2 0.8 copy.61
  (64 shorter events, 3.2 us)
Async XLA Ops:
  6.5 144.8 %copy-start.8 = (f32[1664]{0:T(1024)S(1)}, f32[1664]{0:T(1024)}, u32[]{:S(2)}) copy-start(f32[1664]{0:T(1024)} %param.18) | copy-start | bytes 19972
  6.5 144.8 %copy-start.7 = (f32[1664]{0:T(1024)S(1)}, f32[1664]{0:T(1024)}, u32[]{:S(2)}) copy-start(f32[1664]{0:T(1024)} %param.19) | copy-start | bytes 19972
  6.5 49.8 %all-gather.19.cloned.1.call-start = ((), (), s32[]{:S(2)}) async-start(), calls=%async_computation.11 | async-start | bytes 1892352 | tf_op jit(solution)/shard_map/all_gather | solution.py:93
  7.3 91.4 %all-gather.11.cloned.1.call-start = ((), (), s32[]{:S(2)}) async-start(), calls=%async_computation.4 | async-start | bytes 4259840 | tf_op jit(solution)/shard_map/all_gather | solution.py:81
  8.0 143.3 %all-gather.13.cloned.1.call-start = ((), (), s32[]{:S(2)}) async-start(), calls=%async_computation.5 | async-start | bytes 7028736 | tf_op jit(solution)/shard_map/all_gather | solution.py:87
  9.8 227.0 %reduce-scatter.4.cloned.1.call-start = ((), (), s32[]{:S(2)}) async-start(), calls=%async_computation.6 | async-start | bytes 4259840 | tf_op jit(solution)/shard_map/reduce_scatter | solution.py:96
  98.7 52.6 %copy-start.1 = (bf16[1024,1664]{0,1:T(8,128)(2,1)S(1)}, bf16[1024,1664]{0,1:T(8,128)(2,1)}, u32[]{:S(2)}) copy-start(bf16[1024,1664]{0,1:T(8,128)(2,1)} %all-gather.11.cloned.1.call-done) | copy-start | bytes 10223620
  104.3 57.2 %copy-start.5 = (s32[1024]{0:T(1024)S(1)}, s32[1024]{0:T(1024)}, u32[]{:S(2)}) copy-start(s32[1024]{0:T(1024)} %param.17) | copy-start | bytes 12292
  161.5 32.3 %copy-start.4 = (bf16[1664,416]{1,0:T(8,128)(2,1)S(1)}, bf16[1664,416]{1,0:T(8,128)(2,1)}, u32[]{:S(2)}) copy-start(bf16[1664,416]{1,0:T(8,128)(2,1)} %reshape.125) | copy-start | bytes 4153348
  193.8 42.9 %copy-start.3 = (bf16[1024,416]{0,1:T(8,128)(2,1)S(1)}, bf16[1024,416]{0,1:T(8,128)(2,1)}, u32[]{:S(2)}) copy-start(bf16[1024,416]{0,1:T(8,128)(2,1)} %param.16) | copy-start | bytes 2555908
  197.5 92.0 %all-gather.21.cloned.1.call-start = ((), (), s32[]{:S(2)}) async-start(), calls=%async_computation.12 | async-start | bytes 7569408 | tf_op jit(solution)/shard_map/all_gather | solution.py:105
  198.1 143.3 %all-gather.23.cloned.1.call-start = ((), (), s32[]{:S(2)}) async-start(), calls=%async_computation.13 | async-start | bytes 7569408 | tf_op jit(solution)/shard_map/all_gather | solution.py:111
  198.7 185.0 %all-gather.15.cloned.1.call-start = ((), (), s32[]{:S(2)}) async-start(), calls=%async_computation.7 | async-start | bytes 4259840 | tf_op jit(solution)/shard_map/all_gather | solution.py:100
  239.2 229.5 %reduce-scatter.6.cloned.1.call-start = ((), (), s32[]{:S(2)}) async-start(), calls=%async_computation.8 | async-start | bytes 4259840 | tf_op jit(solution)/shard_map/reduce_scatter | solution.py:114
  350.2 39.3 %copy-start.9 = (f32[1664]{0:T(1024)S(1)}, f32[1664]{0:T(1024)}, u32[]{:S(2)}) copy-start(f32[1664]{0:T(1024)} %param.23) | copy-start | bytes 19972
  350.2 39.3 %copy-start.10 = (f32[1664]{0:T(1024)S(1)}, f32[1664]{0:T(1024)}, u32[]{:S(2)}) copy-start(f32[1664]{0:T(1024)} %param.22) | copy-start | bytes 19972
  383.7 5.9 copy-start.2
  386.4 32.5 %slice-start = ((s8[6815744]{0:T(1024)(128)(4,1)}), s8[4194304]{0:T(1024)(128)(4,1)S(1)}, s32[]{:S(2)}) async-start(s8[6815744]{0:T(1024)(128)(4,1)} %bitcast.77), calls=%async_computation.14 | async-start | bytes 8388608
  389.5 29.4 %slice-start.1 = ((s8[6815744]{0:T(1024)(128)(4,1)}), s8[2621440]{0:T(1024)(128)(4,1)S(1)}, s32[]{:S(2)}) async-start(s8[6815744]{0:T(1024)(128)(4,1)} %bitcast.77), calls=%async_computation.15 | async-start | bytes 5242880
  419.0 49.7 %copy-start = (bf16[1024,416]{0,1:T(8,128)(2,1)S(1)}, bf16[1024,416]{0,1:T(8,128)(2,1)}, u32[]{:S(2)}) copy-start(bf16[1024,416]{0,1:T(8,128)(2,1)} %add_convert_fusion.1) | copy-start | bytes 2555908
  427.7 93.0 %all-gather.17.cloned.1.call-start = ((), (), s32[]{:S(2)}) async-start(), calls=%async_computation.9 | async-start | bytes 7028736 | tf_op jit(solution)/shard_map/all_gather | solution.py:135
  428.5 119.1 %reduce-scatter.8.cloned.1.call-start = ((), (), s32[]{:S(2)}) async-start(), calls=%async_computation.10 | async-start | bytes 1064960 | tf_op jit(solution)/shard_map/reduce_scatter | solution.py:138
  520.7 6.4 %copy-start.6 = (s32[256,1]{0,1:T(1,128)S(1)}, s32[256,1]{0,1:T(1,128)}, u32[]{:S(2)}) copy-start(s32[256,1]{0,1:T(1,128)} %param.29) | copy-start | bytes 3076
Sparse Core Ops, SparseCore 0:
  9.6 46.7 all-gather.18
  58.0 40.5 all-gather.10
  100.9 50.3 all-gather.12
  197.6 39.0 reduce-scatter.3
  238.8 50.6 all-gather.20
  291.6 49.7 all-gather.22
  343.1 40.5 all-gather.14
  427.9 40.7 reduce-scatter.5
  471.0 49.7 all-gather.16
  527.2 20.2 reduce-scatter.7
where the time goes:
time: 598 us; the launch traced here: 590 us
  waiting for transfers between devices  399 us (67%)
  matrix products  83.4 us (14%)
  local copies, waits for them, and re-layouts  46.7 us (8%)
  blocking collectives  26.6 us (4%)
  other arithmetic  18.5 us (3%)
  between operations  14 us (2%)
    all_gather x1, waiting for transfers between devices, body(): lax.all_gather(up_weight, 'gy', axis=0, tiled=True)  50.2 us
    all_gather x1, waiting for transfers between devices, body(): lax.all_gather(query_key_value, 'gy', axis=1, tiled=True)  47 us
    all_gather x1, waiting for transfers between devices, body(): lax.all_gather(project_out, 'gy', axis=1, tiled=True)  46.5 us
    all_gather x1, waiting for transfers between devices, body(): lax.all_gather(down_weight, 'gy', axis=1, tiled=True)  43.3 us
    all_gather x1, waiting for transfers between devices, body(): lax.all_gather(merge_weight, 'gy', axis=2, tiled=True)  40.9 us
    reduce_scatter x1, waiting for transfers between devices, body(): lax.psum_scatter(down_terms.astype(jnp.bfloat16), 'gx', scatter_dimension...  38.6 us
    all_gather x1, waiting for transfers between devices, body(): full_rows = lax.all_gather(tokens, 'gx', axis=1, tiled=True)  38.4 us
    reduce_scatter x1, waiting for transfers between devices, body(): lax.psum_scatter(out_terms.astype(jnp.bfloat16), 'gx', scatter_dimension=...  38 us
  transfers between devices with their start and end apart: 10, of which 10 were waited for; matrix products, arithmetic and copies ran while one was open for 6% of the time, Pallas kernels for 0%

commit v1 on v0

--- a/solution.py
+++ b/solution.py
@@ -6,6 +6,12 @@
 HEAD = 104
 IMG_W = 16
 EPSILON = 1e-06
+
+
+def in_order(blocks, dim):
+    blocks = jnp.moveaxis(blocks, 0, dim)
+    shape = blocks.shape
+    return blocks.reshape(*shape[:dim], shape[dim] * shape[dim + 1], *shape[dim + 2 :])
 
 
 def normalize_rows(values, gain, bias):
@@ -78,7 +84,19 @@
     tok_rows = tokens.shape[0]
     feature_cols = tokens.shape[1]
     features = feature_cols * lax.axis_size("gx")
-    full_rows = lax.all_gather(tokens, "gx", axis=1, tiled=True)
+    length = lax.axis_size("gx")
+    pairs = [(i, (i + 1) % length) for i in range(length)]
+    back = [(b, a) for a, b in pairs]
+    lower, upper_2 = ([], [])
+    for step in range(length - 1):
+        if step % 2 == 0:
+            lower.append(lax.ppermute(lower[-1] if lower else tokens, "gx", pairs))
+        else:
+            upper_2.append(lax.ppermute(upper_2[-1] if upper_2 else tokens, "gx", back))
+    blocks_2 = jnp.stack([*lower[::-1], tokens, *upper_2])
+    shift = lax.axis_index("gx") - len(lower)
+    blocks_2 = blocks_2[(jnp.arange(length) - shift) % length]
+    full_rows = in_order(blocks_2, 1)
     normed = normalize_rows(full_rows, first_gain, first_bias).astype(jnp.bfloat16)
     columns = normed
     qkv = jnp.einsum(

time: 598 us -> 557 us (0.931)
  waiting for transfers between devices: 399 us -> 339 us
  local copies, waits for them, and re-layouts: 46.7 us -> 56.1 us
    all_gather x1, waiting for transfers between devices: 46.5 us -> 0.02 us  [body(): lax.all_gather(project_out, 'gy', axis=1, tiled=True)]
    ppermute x0 -> x3, waiting for transfers between devices: none -> 39.2 us  [the longest x2 39.2 us: body(): lower.append(lax.ppermute(lower[-1] if lower else tokens, 'gx', pairs))]
    all_gather x1 -> x0, waiting for transfers between devices: 38.4 us -> none  [body(): full_rows = lax.all_gather(tokens, 'gx', axis=1, tiled=True)]
    all_gather x1, waiting for transfers between devices: 47 us -> 33.3 us  [body(): lax.all_gather(query_key_value, 'gy', axis=1, tiled=True)]
    convert_element_type x0 -> x1, local copies, waits for them, and re-layouts: none -> 7.65 us  [normalize_rows(): values = values.astype(jnp.float32)]
    unnamed x32 -> x28, local copies, waits for them, and re-layouts: 24 us -> 23 us
  transfers between devices with their start and end apart: 10 -> 12, of which waited for: 10 -> 10; matrix products, arithmetic and copies ran while one was open for 6% -> 9% of each run, Pallas kernels for 0% -> 0%
where the time goes in v1:
time: 557 us; the launch traced here: 548 us
  waiting for transfers between devices  339 us (61%)
  matrix products  85.3 us (15%)
  local copies, waits for them, and re-layouts  56.1 us (10%)
  blocking collectives  26.6 us (5%)
  other arithmetic  21 us (4%)
  between operations  13.9 us (2%)
    all_gather x1, waiting for transfers between devices, body(): lax.all_gather(up_weight, 'gy', axis=0, tiled=True)  50.3 us
    all_gather x1, waiting for transfers between devices, body(): lax.all_gather(down_weight, 'gy', axis=1, tiled=True)  43.4 us
    all_gather x1, waiting for transfers between devices, body(): lax.all_gather(merge_weight, 'gy', axis=2, tiled=True)  40.9 us
    ppermute x2, waiting for transfers between devices, body(): lower.append(lax.ppermute(lower[-1] if lower else tokens, 'gx', pairs))  39.2 us
    reduce_scatter x1, waiting for transfers between devices, body(): lax.psum_scatter(down_terms.astype(jnp.bfloat16), 'gx', scatter_dimension...  38.6 us
    reduce_scatter x1, waiting for transfers between devices, body(): lax.psum_scatter(out_terms.astype(jnp.bfloat16), 'gx', scatter_dimension=...  38 us
    all_gather x1, waiting for transfers between devices, body(): lax.all_gather(query_key_value, 'gy', axis=1, tiled=True)  33.3 us
    all_gather x1, waiting for transfers between devices, body(): resid_rows = lax.all_gather(first_resid, 'gx', axis=1, tiled=True)  33.1 us
  transfers between devices with their start and end apart: 12, of which 10 were waited for; matrix products, arithmetic and copies ran while one was open for 9% of the time, Pallas kernels for 0%

profile of v1, /device:TPU:1, one launch (start us, length us, event | category | flops | bytes accessed | tf_op | source)
XLA Modules:
  0.0 548.1 jit_solution(9761542293915147499)
XLA Ops:
  6.5 0.7 all-gather.16.cloned.1.call-update
  7.3 1.7 copy.28
  9.1 2.5 collective-permute-start
  11.6 2.2 collective-permute-start.2
  13.8 18.8 %collective-permute-done = bf16[1024,416]{0,1:T(8,128)(2,1)S(1)} collective-permute-done((bf16[1024,416]{0,1:T(8,128)(2,1)}, bf16[1024,416]{0,1:T(8,128)(2,1)S(1)}, u32[]{:S(2)}, u32[]{:S(2)}) %collective-permute-start) | collective-permute-done | bytes 852000 | tf_op jit(solution)/shard_map/ppermute | solution.py:93
  32.6 20.4 %collective-permute-done.1 = bf16[1024,416]{0,1:T(8,128)(2,1)S(1)} collective-permute-done((bf16[1024,416]{0,1:T(8,128)(2,1)S(1)}, bf16[1024,416]{0,1:T(8,128)(2,1)S(1)}, u32[]{:S(2)}, u32[]{:S(2)}) %collective-permute-start.1) | collective-permute-done | bytes 852000 | tf_op jit(solution)/shard_map/ppermute | solution.py:93
  53.1 3.0 pad_maximum_fusion
  56.1 2.7 gather_fusion
  58.8 3.6 convert_element_type.103
  62.3 7.7 %copy.27 = f32[1024,1664]{1,0:T(8,128)} copy(f32[1024,1664]{0,1:T(8,128)} %bitcast.85) | data formatting | bytes 13631488 | tf_op jit(solution)/shard_map/convert_element_type | solution.py:18
  70.6 0.9 multiply_reduce_fusion
  71.6 2.7 reshape.191
  74.4 33.3 %all-gather.10.cloned.1.call-done = bf16[3,1664,416]{2,0,1:T(4,128)(2,1)} async-done(((bf16[3,52,416]{2,0,1:T(4,128)(2,1)}), bf16[3,1664,416]{2,0,1:T(4,128)(2,1)}) %all-gather.10.cloned.1.call-update) | async-done | bytes 4153360 | tf_op jit(solution)/shard_map/all_gather | solution.py:105
  107.6 10.7 %convert_bitcast_fusion = bf16[3,1024,416]{1,2,0:T(8,128)(2,1)S(1)} fusion(bf16[3,1664,416]{2,0,1:T(4,128)(2,1)} %all-gather.10.cloned.1.call-done, f32[1024,1664]{1,0:T(8,128)} %copy.27, f32[1664]{0:T(1024)S(1)} %copy-done.5, f32[1664]{0:T(1024)S(1)} %copy-done.6, f32[1024]{0:T(1024)S(1)} %add_rsqrt_fusion.2, f32[1024]{0:T(1024)S(1)} %broadcast_multiply_fusion.2), kind=kOutput, calls=%fused_computation.76 | convolution fusion | flops 4262821888 | bytes 13546496 | tf_op jit(solution)/shard_map/td,kdc->ktc/dot_general | solution.py:102
  118.4 1.5 fusion.125
  119.9 30.2 %while.10 = (s32[]{:T(128)}, bf16[2,512,4,104]{1,3,2,0:T(8,128)(2,1)}, s32[2]{0:T(128)S(1)}, s32[1024]{0:T(1024)S(1)}, bf16[1024,4,104]{0,2,1:T(8,128)(2,1)}, /*...) while((s32[]{:T(128)}, ...), condition=%wide.region_8.9_spmd, body=%wide.region_5.8_spmd.sunk | while | flops 885736448 | bytes 20409008 | solution.py:64
  121.8 7.6 %fusion.153 = (f32[4,512]{1,0:T(4,128)S(1)}, f32[4,512,1024]{2,1,0:T(8,128)}) fusion(pred[512,1024]{1,0:T(8,128)(4,1)S(1)} %broadcast_compare_fusion.2, bf16[1024,4,104]{0,2,1:T(8,128)(2,1)} %get-tuple-element.142, bf16[1024,4,104]{0,2,1:T(8,128)(2,1)} %get-tuple-element.141, s32[]{:T(128)S(6)} %select_n.82), kind=kOutput, calls=%fused_computation.141.clone.1 | convolution fusion | flops 444597248 | bytes 10199044 | tf_op jit(solution)/shard_map/while/body/eval_jaxpr/sub | solution.py:58
  129.4 5.7 %fusion.154 = bf16[2,512,4,104]{1,3,2,0:T(8,128)(2,1)} fusion(bf16[2,512,4,104]{1,3,2,0:T(8,128)(2,1)} %get-tuple-element.127, s32[]{:T(128)} %get-tuple-element.126, bf16[1024,4,104]{0,2,1:T(8,128)(2,1)S(1)} %get-tuple-element.143, f32[4,512,1024]{2,1,0:T(8,128)} %get-tuple-element.113, f32[4,512]{1,0:T(4,128)S(1)} %get-tuple-element.114), kind=kOutput, calls=%fused_computation.13.clone.1 | convolution fusion | flops 440614912 | bytes 9675264 | tf_op jit(solution)/shard_map/while/body/eval_jaxpr/hqk,khe->qhe/dot_general | solution.py:60
  136.8 7.6 %fusion.153 = (f32[4,512]{1,0:T(4,128)S(1)}, f32[4,512,1024]{2,1,0:T(8,128)}) fusion(pred[512,1024]{1,0:T(8,128)(4,1)S(1)} %broadcast_compare_fusion.2, bf16[1024,4,104]{0,2,1:T(8,128)(2,1)} %get-tuple-element.142, bf16[1024,4,104]{0,2,1:T(8,128)(2,1)} %get-tuple-element.141, s32[]{:T(128)S(6)} %select_n.82), kind=kOutput, calls=%fused_computation.141.clone.1 | convolution fusion | flops 444597248 | bytes 10199044 | tf_op jit(solution)/shard_map/while/body/eval_jaxpr/sub | solution.py:58
  144.4 5.7 %fusion.154 = bf16[2,512,4,104]{1,3,2,0:T(8,128)(2,1)} fusion(bf16[2,512,4,104]{1,3,2,0:T(8,128)(2,1)} %get-tuple-element.127, s32[]{:T(128)} %get-tuple-element.126, bf16[1024,4,104]{0,2,1:T(8,128)(2,1)S(1)} %get-tuple-element.143, f32[4,512,1024]{2,1,0:T(8,128)} %get-tuple-element.113, f32[4,512]{1,0:T(4,128)S(1)} %get-tuple-element.114), kind=kOutput, calls=%fused_computation.13.clone.1 | convolution fusion | flops 440614912 | bytes 9675264 | tf_op jit(solution)/shard_map/while/body/eval_jaxpr/hqk,khe->qhe/dot_general | solution.py:60
  150.1 2.0 copy.30
  152.3 3.7 convolution_convert_fusion
  157.2 38.0 %reduce-scatter.4.cloned.1.call-done = bf16[1024,416]{0,1:T(8,128)(2,1)} async-done(((bf16[1024,1664]{0,1:T(8,128)(2,1)}), bf16[1024,416]{0,1:T(8,128)(2,1)}) %reduce-scatter.4.cloned.1.call-update) | async-done | bytes 851984 | tf_op jit(solution)/shard_map/reduce_scatter | solution.py:114
  195.2 2.4 add_convert_fusion.2
  197.7 50.3 %all-gather.18.cloned.1.call-done = bf16[32,52,2048]{2,1,0:T(8,128)(2,1)} async-done(((bf16[1,52,2048]{2,1,0:T(8,128)(2,1)}), bf16[32,52,2048]{2,1,0:T(8,128)(2,1)}) %all-gather.18.cloned.1.call-update) | async-done | bytes 6815760 | tf_op jit(solution)/shard_map/all_gather | solution.py:123
  248.0 8.6 %reshape.193 = bf16[1664,2048]{1,0:T(8,128)(2,1)} reshape(bf16[32,52,2048]{2,1,0:T(8,128)(2,1)} %all-gather.18.cloned.1.call-done) | data formatting | bytes 13631488
  256.5 43.4 %all-gather.20.cloned.1.call-done = bf16[32,52,2048]{2,1,0:T(8,128)(2,1)} async-done(((bf16[1,52,2048]{2,1,0:T(8,128)(2,1)}), bf16[32,52,2048]{2,1,0:T(8,128)(2,1)}) %all-gather.20.cloned.1.call-update) | async-done | bytes 6815760 | tf_op jit(solution)/shard_map/all_gather | solution.py:129
  299.9 9.0 %reshape.195 = bf16[1664,2048]{1,0:T(8,128)(2,1)} reshape(bf16[32,52,2048]{2,1,0:T(8,128)(2,1)} %all-gather.20.cloned.1.call-done) | data formatting | bytes 13631488
  308.9 33.1 %all-gather.12.cloned.1.call-done = bf16[1024,1664]{0,1:T(8,128)(2,1)} async-done(((bf16[1024,416]{0,1:T(8,128)(2,1)}), bf16[1024,1664]{0,1:T(8,128)(2,1)}) %all-gather.12.cloned.1.call-update) | async-done | bytes 3407888 | tf_op jit(solution)/shard_map/all_gather | solution.py:118
  342.0 2.7 convert_reduce_fusion
  344.7 3.1 fusion.36
  347.8 29.2 %fusion.143 = bf16[1024,2048]{1,0:T(8,128)(2,1)S(1)} fusion(bf16[1664,2048]{1,0:T(8,128)(2,1)} %reshape.193, bf16[1024,1664]{0,1:T(8,128)(2,1)S(1)} %copy-done.1, f32[1664]{0:T(1024)S(1)} %copy-done.7, f32[1664]{0:T(1024)S(1)} %copy-done.8, f32[1024]{0:T(1024)S(1)} %add_rsqrt_fusion.1, f32[1024]{0:T(1024)S(1)} %broadcast_multiply_fusion.1), kind=kOutput, calls=%fused_computation.28.clone.clone.clone.clone.1 | convolution fusion | flops 7125860352 | bytes 14439424 | tf_op jit(solution)/shard_map/dot_general | solution.py:121
  377.1 8.7 %fusion.46 = bf16[1024,1664]{0,1:T(8,128)(2,1)} fusion(bf16[1664,2048]{1,0:T(8,128)(2,1)S(1)} %bitcast.88, bf16[1024,2048]{1,0:T(8,128)(2,1)S(1)} %fusion.143), kind=kOutput, calls=%fused_computation.57 | convolution fusion | flops 6981025792 | bytes 14417920 | tf_op jit(solution)/shard_map/dot_general | solution.py:127
  385.9 0.7 all-gather.14.cloned.1.call-update
  386.6 0.8 dynamic_slice.16
  387.4 0.8 dynamic_slice.17
  388.2 38.6 %reduce-scatter.6.cloned.1.call-done = bf16[1024,416]{0,1:T(8,128)(2,1)} async-done(((bf16[1024,1664]{0,1:T(8,128)(2,1)}), bf16[1024,416]{0,1:T(8,128)(2,1)}) %reduce-scatter.6.cloned.1.call-update) | async-done | bytes 851984 | tf_op jit(solution)/shard_map/reduce_scatter | solution.py:132
  426.8 1.5 convert_reduce_fusion.2
  428.3 6.6 %all-reduce = (f32[1024]{0:T(1024)S(1)}, f32[1024]{0:T(1024)S(1)}) all-reduce(f32[1024]{0:T(1024)S(1)} %get-tuple-element.44, f32[1024]{0:T(1024)S(1)} %get-tuple-element.43), channel_id=1, replica_groups=mesh['gx'=4,'gy'=32] {'gx'}, use_global_device_ids=true, to_apply=%region_16.17 | all-reduce | flops 2048 | bytes 16384 | tf_op jit(solution)/shard_map/psum | solution.py:136
  435.0 1.6 fusion.82
  436.6 0.8 copy.31
  438.0 40.9 %all-gather.14.cloned.1.call-done = bf16[4,416,1664]{1,0,2:T(4,128)(2,1)} async-done(((bf16[4,416,52]{1,0,2:T(4,128)(2,1)}), bf16[4,416,1664]{1,0,2:T(4,128)(2,1)}) %all-gather.14.cloned.1.call-update) | async-done | bytes 5537808 | tf_op jit(solution)/shard_map/all_gather | solution.py:153
  478.9 6.3 %fusion.72 = bf16[256,1664]{0,1:T(8,128)(2,1)} fusion(bf16[256,4,416]{2,0,1:T(8,128)(2,1)S(1)} %bitcast.93, bf16[4,416,1664]{1,0,2:T(4,128)(2,1)} %all-gather.14.cloned.1.call-done), kind=kOutput, calls=%fused_computation.72 | convolution fusion | flops 1418100736 | bytes 7241728 | tf_op jit(solution)/shard_map/pkf,kfc->pc/dot_general | solution.py:150
  486.2 19.4 %reduce-scatter.8.cloned.1.call-done = bf16[256,416]{0,1:T(8,128)(2,1)} async-done(((bf16[256,1664]{0,1:T(8,128)(2,1)}), bf16[256,416]{0,1:T(8,128)(2,1)}) %reduce-scatter.8.cloned.1.call-update) | async-done | bytes 213008 | tf_op jit(solution)/shard_map/reduce_scatter | solution.py:156
  505.6 1.1 copy.35
  506.7 13.6 %scatter_fusion = bf16[32,16,416]{2,1,0:T(8,128)(2,1)S(1)} fusion(bf16[32,16,416]{2,1,0:T(8,128)(2,1)S(1)} %broadcast_in_dim.19, s32[256]{0:T(256)S(1)} %bitcast.86, bf16[256,416]{1,0:T(8,128)(2,1)S(1)} %copy.35), kind=kCustom, calls=%fused_computation.1 | custom fusion | bytes 641024 | tf_op jit(solution)/shard_map/scatter | solution.py:169
  520.3 20.0 %all_to_all.5 = bf16[32,16,416]{2,1,0:T(8,128)(2,1)S(1)} all-to-all(bf16[32,16,416]{2,1,0:T(8,128)(2,1)S(1)} %scatter_fusion), channel_id=1, replica_groups=mesh['gx'=4,'gy'=32] {'gy'}, dimensions={0} | all-to-all | bytes 851968 | tf_op jit(solution)/shard_map/all_to_all | solution.py:171
  540.3 0.8 copy.59
  (69 shorter events, 6.1 us)
Async XLA Ops:
  6.5 65.1 %all-gather.16.cloned.1.call-start = ((), (), s32[]{:S(2)}) async-start(), calls=%async_computation.10 | async-start | bytes 1892352 | tf_op jit(solution)/shard_map/all_gather | solution.py:111
  7.3 100.4 %all-gather.10.cloned.1.call-start = ((), (), s32[]{:S(2)}) async-start(), calls=%async_computation.4 | async-start | bytes 7028736 | tf_op jit(solution)/shard_map/all_gather | solution.py:105
  9.0 186.1 %reduce-scatter.4.cloned.1.call-start = ((), (), s32[]{:S(2)}) async-start(), calls=%async_computation.5 | async-start | bytes 4259840 | tf_op jit(solution)/shard_map/reduce_scatter | solution.py:114
  9.1 23.5 %collective-permute-start = (bf16[1024,416]{0,1:T(8,128)(2,1)}, bf16[1024,416]{0,1:T(8,128)(2,1)S(1)}, u32[]{:S(2)}, u32[]{:S(2)}) collective-permute-start(bf16[1024,416]{0,1:T(8,128)(2,1)} %param.16), channel_id=1, source_target_pairs={{0,32},{32,64},{64,96},{96,0},{1,33},{33,65},{65,97},{97,1},{2,34}... | collective-permute-start | bytes 2555912 | tf_op jit(solution)/shard_map/ppermute | solution.py:93
  11.6 21.0 %collective-permute-start.2 = (bf16[1024,416]{0,1:T(8,128)(2,1)}, bf16[1024,416]{0,1:T(8,128)(2,1)S(1)}, u32[]{:S(2)}, u32[]{:S(2)}) collective-permute-start(bf16[1024,416]{0,1:T(8,128)(2,1)} %param.16), channel_id=1, source_target_pairs={{32,0},{64,32},{96,64},{0,96},{33,1},{65,33},{97,65},{1,97},{34,2}... | collective-permute-start | bytes 2555912 | tf_op jit(solution)/shard_map/ppermute | solution.py:95
  32.6 20.5 %collective-permute-start.1 = (bf16[1024,416]{0,1:T(8,128)(2,1)S(1)}, bf16[1024,416]{0,1:T(8,128)(2,1)S(1)}, u32[]{:S(2)}, u32[]{:S(2)}) collective-permute-start(bf16[1024,416]{0,1:T(8,128)(2,1)S(1)} %collective-permute-done), channel_id=1, source_target_pairs={{0,32},{32,64},{64,96},{96,0},{1,33},{33,65},{65,97},{97,1},{2,34}... | collective-permute-start | bytes 2555912 | tf_op jit(solution)/shard_map/ppermute | solution.py:93
  70.0 37.6 %copy-start.5 = (f32[1664]{0:T(1024)S(1)}, f32[1664]{0:T(1024)}, u32[]{:S(2)}) copy-start(f32[1664]{0:T(1024)} %param.19) | copy-start | bytes 19972
  70.0 37.6 %copy-start.6 = (f32[1664]{0:T(1024)S(1)}, f32[1664]{0:T(1024)}, u32[]{:S(2)}) copy-start(f32[1664]{0:T(1024)} %param.18) | copy-start | bytes 19972
  74.3 45.5 %copy-start.3 = (s32[1024]{0:T(1024)S(1)}, s32[1024]{0:T(1024)}, u32[]{:S(2)}) copy-start(s32[1024]{0:T(1024)} %param.17) | copy-start | bytes 12292
  152.3 42.9 %copy-start.2 = (bf16[1024,416]{0,1:T(8,128)(2,1)S(1)}, bf16[1024,416]{0,1:T(8,128)(2,1)}, u32[]{:S(2)}) copy-start(bf16[1024,416]{0,1:T(8,128)(2,1)} %param.16) | copy-start | bytes 2555908
  156.0 92.0 %all-gather.18.cloned.1.call-start = ((), (), s32[]{:S(2)}) async-start(), calls=%async_computation.11 | async-start | bytes 7569408 | tf_op jit(solution)/shard_map/all_gather | solution.py:123
  156.6 143.4 %all-gather.20.cloned.1.call-start = ((), (), s32[]{:S(2)}) async-start(), calls=%async_computation.12 | async-start | bytes 7569408 | tf_op jit(solution)/shard_map/all_gather | solution.py:129
  157.1 184.8 %all-gather.12.cloned.1.call-start = ((), (), s32[]{:S(2)}) async-start(), calls=%async_computation.6 | async-start | bytes 4259840 | tf_op jit(solution)/shard_map/all_gather | solution.py:118
  197.6 229.2 %reduce-scatter.6.cloned.1.call-start = ((), (), s32[]{:S(2)}) async-start(), calls=%async_computation.7 | async-start | bytes 4259840 | tf_op jit(solution)/shard_map/reduce_scatter | solution.py:132
  308.9 38.9 %copy-start.7 = (f32[1664]{0:T(1024)S(1)}, f32[1664]{0:T(1024)}, u32[]{:S(2)}) copy-start(f32[1664]{0:T(1024)} %param.23) | copy-start | bytes 19972
  308.9 38.9 %copy-start.8 = (f32[1664]{0:T(1024)S(1)}, f32[1664]{0:T(1024)}, u32[]{:S(2)}) copy-start(f32[1664]{0:T(1024)} %param.22) | copy-start | bytes 19972
  342.0 5.9 %copy-start.1 = (bf16[1024,1664]{0,1:T(8,128)(2,1)S(1)}, bf16[1024,1664]{0,1:T(8,128)(2,1)}, u32[]{:S(2)}) copy-start(bf16[1024,1664]{0,1:T(8,128)(2,1)} %all-gather.12.cloned.1.call-done) | copy-start | bytes 10223620
  344.7 32.4 %slice-start = ((s8[6815744]{0:T(1024)(128)(4,1)}), s8[4194304]{0:T(1024)(128)(4,1)S(1)}, s32[]{:S(2)}) async-start(s8[6815744]{0:T(1024)(128)(4,1)} %bitcast.87), calls=%async_computation.13 | async-start | bytes 8388608
  347.8 29.3 %slice-start.1 = ((s8[6815744]{0:T(1024)(128)(4,1)}), s8[2621440]{0:T(1024)(128)(4,1)S(1)}, s32[]{:S(2)}) async-start(s8[6815744]{0:T(1024)(128)(4,1)} %bitcast.87), calls=%async_computation.14 | async-start | bytes 5242880
  377.1 49.7 %copy-start = (bf16[1024,416]{0,1:T(8,128)(2,1)S(1)}, bf16[1024,416]{0,1:T(8,128)(2,1)}, u32[]{:S(2)}) copy-start(bf16[1024,416]{0,1:T(8,128)(2,1)} %add_convert_fusion.2) | copy-start | bytes 2555908
  385.8 93.0 %all-gather.14.cloned.1.call-start = ((), (), s32[]{:S(2)}) async-start(), calls=%async_computation.8 | async-start | bytes 7028736 | tf_op jit(solution)/shard_map/all_gather | solution.py:153
  386.6 119.0 %reduce-scatter.8.cloned.1.call-start = ((), (), s32[]{:S(2)}) async-start(), calls=%async_computation.9 | async-start | bytes 1064960 | tf_op jit(solution)/shard_map/reduce_scatter | solution.py:156
  478.9 6.4 %copy-start.4 = (s32[256,1]{0,1:T(1,128)S(1)}, s32[256,1]{0,1:T(1,128)}, u32[]{:S(2)}) copy-start(s32[256,1]{0,1:T(1,128)} %param.29) | copy-start | bytes 3076
Sparse Core Ops, SparseCore 0:
  9.6 46.5 all-gather.15
  58.5 49.1 all-gather.9
  156.1 39.0 reduce-scatter.3
  197.3 50.6 all-gather.17
  250.1 49.7 all-gather.19
  301.4 40.4 all-gather.11
  386.0 40.7 reduce-scatter.5
  429.1 49.7 all-gather.13
  485.4 20.1 reduce-scatter.7
